TPU v7x, 128 devices: a whole 4x4x4 slice. The times are simulated.
128 devices in a mesh: dp: 4 (over y_hi, core), head: 4 (over x), ctx: 8 (over z, y_lo).
Axes of the slice: x: 4, y: 4 (y_hi: 2, y_lo: 2; y = y_hi * 2 + y_lo), z: 4, core: 2. Of those that a mesh axis runs over, the one named last changes fastest.
Arguments:
- video: bfloat16 [16, 64, 24576], P('dp', 'head', 'ctx'), parts along dimension 0, may hold values from -6 to 6
- cache: bfloat16 [8, 64, 24576], P('dp', 'head', 'ctx'), parts along dimension 0, may hold values from -6 to 6
- conv_weight: bfloat16 [3, 3, 288, 192], replicated, may hold values from -0.125 to 0.125
- conv_bias: float32 [192], replicated, may hold values from -3 to 3
- down_weight: bfloat16 [768, 192], replicated, may hold values from -0.21875 to 0.21875
- patch_weight: bfloat16 [768, 5120], P(None, ('head', 'ctx')), may hold values from -0.21875 to 0.21875
- step_index: int32 [4], P('dp'), parts along dimension 0, may hold values from 0 to 999
- mod_weight: bfloat16 [256, 10240], P(None, ('head', 'ctx')), may hold values from -1 to 1
- qkv_weight: bfloat16 [5120, 20, 3, 128], P('ctx', 'head'), may hold values from -0.078125 to 0.078125
Outputs:
- attended: bfloat16 [16384, 2560], P(('dp', 'ctx'), 'head'), parts along dimension 0
There are 4 independent parts, one for each index of `dp`. A program takes and returns all parts, laid end to end along the dimension named above; an argument that names none is the same for every part. Nothing has to cross between parts.
All inputs are finite; a program needn't handle non-finite values.
Results may differ from a plain program's by a relative error of at most 0.015.
The roundings to bfloat16 on the way count: a program that leaves them out, or rounds other values in their place, can miss the bound.
Values may be sent and summed in bfloat16 or wider, within the bound.
No kernel may reach another device: no remote copies, remote signals or barrier semaphores. Data moves between devices by JAX's collectives and lax.ppermute only.
A program may use at most 128 MiB of HBM per device.

v0:
```python
import jax
import jax.numpy as jnp
from jax import lax
from jax.sharding import PartitionSpec as P

D = 5120
HDIM = 128
FREQ = 256


def with_halo(cells, sides, width):
    for axis, dim in sides:
        count = lax.axis_size(axis)
        ends = count - 1
        head = lax.slice_in_dim(cells, 0, width, axis=dim)
        tail = lax.slice_in_dim(cells, cells.shape[dim] - width, cells.shape[dim], axis=dim)
        cells = jnp.concatenate(
            [
                lax.ppermute(tail, axis, [(i, (i + 1) % count) for i in range(ends)]),
                cells,
                lax.ppermute(head, axis, [((i + 1) % count, i) for i in range(ends)]),
            ],
            axis=dim,
        )
    return cells


def silu_act(value):
    return value * jax.nn.sigmoid(value)


def shards(
    video,
    cache,
    conv_weight,
    conv_bias,
    down_weight,
    patch_weight,
    step_index,
    mod_weight,
    qkv_weight,
):
    cin = conv_weight.shape[2] // 3
    cmid = conv_weight.shape[3]
    frame_count = video.shape[0]
    tile_rows = video.shape[1]
    tile_cols = video.shape[2] // cin
    frames = jnp.concatenate([cache, video], 0).reshape(frame_count + 2, tile_rows, tile_cols, cin)
    padded = with_halo(frames, (("head", 1), ("ctx", 2)), 1)
    total = jnp.zeros((frame_count, tile_rows, tile_cols, cmid), jnp.float32)
    for time_tap in range(3):
        for row_tap in range(3):
            slab = padded[time_tap : time_tap + frame_count, row_tap : row_tap + tile_rows]
            stacked = jnp.concatenate(
                [slab[:, :, col_tap : col_tap + tile_cols] for col_tap in range(3)], -1
            )
            total = total + jnp.einsum(
                "fyxc,cd->fyxd",
                stacked,
                conv_weight[time_tap, row_tap],
                preferred_element_type=jnp.float32,
            )
    hidden = silu_act(total + conv_bias).astype(jnp.bfloat16)
    stacked = (
        hidden.reshape(frame_count, tile_rows // 2, 2, tile_cols // 2, 2, cmid)
        .transpose(0, 1, 3, 2, 4, 5)
        .reshape(-1, 4 * cmid)
    )
    reduced = silu_act(jnp.dot(stacked, down_weight, preferred_element_type=jnp.float32)).astype(
        jnp.bfloat16
    )
    reduced = reduced.reshape(frame_count, tile_rows // 2, tile_cols // 2, cmid)
    patches = reduced.reshape(frame_count, tile_rows // 4, 2, tile_cols // 4, 2, cmid).transpose(
        0, 1, 3, 2, 4, 5
    )
    patches = patches.reshape(-1, 4 * cmid)
    half = FREQ // 2
    freqs = jnp.exp(-jnp.log(10000.0) * jnp.arange(half, dtype=jnp.float32) / half)
    angles = step_index[0].astype(jnp.float32) * freqs
    timing = jnp.concatenate([jnp.cos(angles), jnp.sin(angles)]).astype(jnp.bfloat16)
    mod_share = jnp.dot(timing[None, :], mod_weight, preferred_element_type=jnp.float32)[0]
    modulation = lax.all_gather(mod_share, ("head", "ctx"), axis=0, tiled=True)
    scale = modulation[:D]
    shift = modulation[D:]
    embedded = jnp.dot(
        patches,
        lax.all_gather(patch_weight, ("head", "ctx"), axis=1, tiled=True),
        preferred_element_type=jnp.float32,
    )
    inverse = lax.rsqrt(jnp.mean(embedded * embedded, -1, keepdims=True) + 1e-06)
    normed = (embedded * inverse * (1.0 + scale) + shift).astype(jnp.bfloat16)
    gathered = lax.all_gather(normed, "head", axis=0, tiled=True)
    group_rows = gathered.shape[0]
    heads_here = qkv_weight.shape[1]
    out_cols = heads_here * 3 * HDIM
    piece = lax.all_gather(qkv_weight, "ctx", axis=0, tiled=True)
    qkv = jnp.dot(
        gathered, piece.reshape(piece.shape[0], out_cols), preferred_element_type=jnp.float32
    )
    qkv = qkv.astype(jnp.bfloat16).reshape(group_rows, heads_here, 3, HDIM)
    query = qkv[:, :, 0]
    keys = qkv[:, :, 1]
    values = qkv[:, :, 2]
    inv_root = 1.0 / jnp.sqrt(jnp.float32(HDIM))
    best = jnp.full((heads_here, group_rows), -1e30, jnp.float32)
    key_piece = lax.all_gather(keys, "ctx", axis=0, tiled=True)
    value_piece = lax.all_gather(values, "ctx", axis=0, tiled=True)
    scores = (
        jnp.einsum("qhd,khd->hqk", query, key_piece, preferred_element_type=jnp.float32) * inv_root
    )
    new_best = jnp.maximum(best, jnp.max(scores, -1))
    probs = jnp.exp(scores - new_best[..., None])
    denom = jnp.sum(probs, -1)
    accum = jnp.einsum(
        "hqk,khd->hqd", probs.astype(jnp.bfloat16), value_piece, preferred_element_type=jnp.float32
    )
    best, denom, accum = (new_best, denom, accum)
    result = (accum / denom[..., None]).astype(jnp.bfloat16)
    return result.transpose(1, 0, 2).reshape(group_rows, heads_here * HDIM)


def solution(mesh):
    return jax.shard_map(
        shards,
        mesh=mesh,
        in_specs=(
            P("dp", "head", "ctx"),
            P("dp", "head", "ctx"),
            P(),
            P(),
            P(),
            P(None, ("head", "ctx")),
            P("dp"),
            P(None, ("head", "ctx")),
            P("ctx", "head", None, None),
        ),
        out_specs=P(("dp", "ctx"), "head"),
        check_vma=False,
    )
```

profile of v0, /device:TPU:0, one launch (start us, length us, event | category | flops | bytes accessed | tf_op | source)
XLA Modules:
  0.0 923.2 jit_solution(17581543572212077937)
XLA Ops:
  8.3 1.1 constant_dynamic-update-slice_fusion
  10.8 4.1 collective-permute-start
  14.9 1.3 collective-permute-start.1
  18.7 162.8 %all-reduce = f32[10240]{0:T(1024)S(1)} all-reduce(f32[10240]{0:T(1024)S(1)} %dynamic-update-slice), channel_id=1, replica_groups=mesh['dp'=4,'head'=4,'ctx'=8] {'head','ctx'}, use_global_device_ids=true, to_apply=%add | all-reduce | flops 10240 | bytes 81920
  185.5 1.3 collective-permute-start.2
  186.8 1.5 collective-permute-start.3
  189.7 1.9 fusion.81
  191.6 2.3 collective-permute-done.3
  194.0 2.1 fusion.73
  203.3 2.6 multiply_convert_fusion
  209.6 5.9 multiply_reduce_fusion.1
  215.6 1.5 add_convert_fusion
  217.8 3.1 copy.17
  220.9 49.5 %all-gather.10.cloned.1.call-done = bf16[512,5120]{1,0:T(8,128)(2,1)} async-done(((bf16[128,5120]{1,0:T(8,128)(2,1)}), bf16[512,5120]{1,0:T(8,128)(2,1)}) %all-gather.10.cloned.1.call-update) | async-done | bytes 5242896 | tf_op jit(solution)/shard_map/all_gather | solution.py:92
  270.5 381.9 %all-gather.12.cloned.1.call-done = bf16[5120,5,3,128]{0,3,2,1:T(8,128)(2,1)} async-done(((bf16[640,5,3,128]{0,3,2,1:T(8,128)(2,1)}), bf16[5120,5,3,128]{0,3,2,1:T(8,128)(2,1)}) %all-gather.12.cloned.1.call-update) | async-done | bytes 19660816 | tf_op jit(solution)/shard_map/all_gather | solution.py:96
  652.4 17.7 %convolution_convert_fusion = bf16[512,1920]{1,0:T(8,128)(2,1)} fusion(bf16[512,5120]{1,0:T(8,128)(2,1)} %all-gather.10.cloned.1.call-done, bf16[5120,1920]{0,1:T(8,128)(2,1)} %bitcast.113), kind=kOutput, calls=%fused_computation.24 | convolution fusion | flops 10067312640 | bytes 26869760 | tf_op jit(solution)/shard_map/dot_general | solution.py:97
  670.1 2.7 copy.18
  673.7 1.1 copy.33
  675.4 110.9 %all-gather.14.cloned.1.call-done = bf16[4096,5,1,128]{3,0,1,2:T(8,128)(2,1)} async-done(((bf16[512,5,1,128]{3,0,1,2:T(8,128)(2,1)}), bf16[4096,5,1,128]{3,0,1,2:T(8,128)(2,1)}) %all-gather.14.cloned.1.call-update) | async-done | bytes 5242896 | tf_op jit(solution)/shard_map/all_gather | solution.py:106
  786.3 19.0 %multiply_reduce_fusion = (f32[5,512]{1,0:T(8,128)S(1)}, f32[5,512,4096]{2,1,0:T(8,128)}) fusion(bf16[4096,5,1,128]{3,0,1,2:T(8,128)(2,1)} %all-gather.14.cloned.1.call-done, bf16[512,5,3,128]{0,3,2,1:T(8,128)(2,1)S(1)} %bitcast.108), kind=kOutput, calls=%fused_computation.1 | convolution fusion | flops 2705323520 | bytes 47851520 | tf_op jit(solution)/shard_map/qhd,khd->hqk/dot_general | solution.py:109
  805.3 17.3 %fusion = f32[5,512]{1,0:T(8,128)S(1)} fusion(f32[5,512,4096]{2,1,0:T(8,128)} %get-tuple-element.47, f32[5,512]{1,0:T(8,128)S(1)} %broadcast_maximum_fusion), kind=kLoop, calls=%fused_computation.2 | loop fusion | flops 31454720 | bytes 41963520 | tf_op jit(solution)/shard_map/reduce_sum | solution.py:113
  822.7 75.6 %all-gather.16.cloned.1.call-done = bf16[4096,5,1,128]{0,3,1,2:T(8,128)(2,1)} async-done(((bf16[512,5,1,128]{0,3,1,2:T(8,128)(2,1)}), bf16[4096,5,1,128]{0,3,1,2:T(8,128)(2,1)}) %all-gather.16.cloned.1.call-update) | async-done | bytes 5242896 | tf_op jit(solution)/shard_map/all_gather | solution.py:107
  898.2 17.3 %divide_convert_fusion = bf16[512,5,128]{0,2,1:T(8,128)(2,1)S(1)} fusion(bf16[4096,5,1,128]{0,3,1,2:T(8,128)(2,1)} %all-gather.16.cloned.1.call-done, f32[5,512,4096]{2,1,0:T(8,128)} %get-tuple-element.47, f32[5,512]{1,0:T(8,128)S(1)} %broadcast_maximum_fusion, f32[512,5]{0,1:T(8,128)S(1)} %bitcast.112), kind=kOutput, calls=%fused_computation.84 | convolution fusion | flops 2716467200 | bytes 47861760 | tf_op jit(solution)/shard_map/hqk,khd->hqd/dot_general | solution.py:114
  915.6 1.1 copy.22
  (70 shorter events, 22.7 us)
Async XLA Ops:
  6.5 201.9 %copy-start = (bf16[768,192]{0,1:T(8,128)(2,1)S(1)}, bf16[768,192]{0,1:T(8,128)(2,1)}, u32[]{:S(2)}) copy-start(bf16[768,192]{0,1:T(8,128)(2,1)} %param.13) | copy-start | bytes 884740
  6.5 10.4 %copy-start.7 = (u32[128]{0:T(128)S(1)}, u32[128]{0:T(128)}, u32[]{:S(2)}) copy-start(u32[128]{0:T(128)} %constant.27) | copy-start | bytes 1540
  6.5 11.7 %copy-start.4 = (bf16[256,320]{0,1:T(8,128)(2,1)S(1)}, bf16[256,320]{0,1:T(8,128)(2,1)}, u32[]{:S(2)}) copy-start(bf16[256,320]{0,1:T(8,128)(2,1)} %param.16) | copy-start | bytes 491524
  6.5 203.1 %all-gather.8.cloned.1.call-start = ((), (), s32[]{:S(2)}) async-start(), calls=%async_computation | async-start | bytes 8110080 | tf_op jit(solution)/shard_map/all_gather | solution.py:87
  7.3 263.2 %all-gather.10.cloned.1.call-start = ((), (), s32[]{:S(2)}) async-start(), calls=%async_computation.1 | async-start | bytes 6553600 | tf_op jit(solution)/shard_map/all_gather | solution.py:92
  8.3 173.4 %copy-start.3 = (bf16[4,16,3072]{2,1,0:T(8,128)(2,1)S(1)}, bf16[4,16,3072]{2,1,0:T(8,128)(2,1)}, u32[]{:S(2)}) copy-start(bf16[4,16,3072]{2,1,0:T(8,128)(2,1)} %param.9) | copy-start | bytes 1179652
  10.8 172.5 %collective-permute-start = (bf16[6,1,32,96]{3,2,1,0:T(8,128)(2,1)}, bf16[6,1,32,96]{3,2,1,0:T(8,128)(2,1)}, u32[]{:S(2)}, u32[]{:S(2)}) collective-permute-start(bf16[6,1,32,96]{3,2,1,0:T(8,128)(2,1)} %get-tuple-element.35), channel_id=1, source_target_pairs={{0,8},{8,16},{16,24},{1,9},{9,17},{17,25},{2,10},{10,18},{18,26},{... | collective-permute-start | bytes 110600 | tf_op jit(solution)/shard_map/ppermute | solution.py:19
  14.9 169.7 %collective-permute-start.1 = (bf16[6,1,32,96]{3,2,1,0:T(8,128)(2,1)}, bf16[6,1,32,96]{3,2,1,0:T(8,128)(2,1)}, u32[]{:S(2)}, u32[]{:S(2)}) collective-permute-start(bf16[6,1,32,96]{3,2,1,0:T(8,128)(2,1)} %get-tuple-element.34), channel_id=1, source_target_pairs={{8,0},{16,8},{24,16},{9,1},{17,9},{25,17},{10,2},{18,10},{26,18},{... | collective-permute-start | bytes 110600 | tf_op jit(solution)/shard_map/ppermute | solution.py:21
  185.5 4.3 collective-permute-start.2
  186.8 7.2 collective-permute-start.3
  191.6 4.5 copy-start.5
  202.4 0.9 copy-start.6
  215.6 2.2 copy-start.2
  217.1 435.3 %all-gather.12.cloned.1.call-start = ((), (), s32[]{:S(2)}) async-start(), calls=%async_computation.2 | async-start | bytes 22118400 | tf_op jit(solution)/shard_map/all_gather | solution.py:96
  220.9 565.4 %all-gather.14.cloned.1.call-start = ((), (), s32[]{:S(2)}) async-start(), calls=%async_computation.3 | async-start | bytes 5898240 | tf_op jit(solution)/shard_map/all_gather | solution.py:106
  674.8 223.4 %all-gather.16.cloned.1.call-start = ((), (), s32[]{:S(2)}) async-start(), calls=%async_computation.4 | async-start | bytes 5898240 | tf_op jit(solution)/shard_map/all_gather | solution.py:107
  898.2 18.4 %copy-start.1 = (bf16[768,192]{0,1:T(8,128)(2,1)S(1)}, bf16[768,192]{0,1:T(8,128)(2,1)}, u32[]{:S(2)}) copy-start(bf16[768,192]{0,1:T(8,128)(2,1)} %param.13) | copy-start | bytes 884740
Sparse Core Ops, SparseCore 0:
  9.0 188.3 all-gather.7
  217.2 53.2 all-gather.9
  272.1 380.1 all-gather.11
  675.0 111.2 all-gather.13
  787.8 110.4 all-gather.15
where the time goes:
time: 924 us; the launch traced here: 923 us
  waiting for transfers between devices  622 us (67%)
  blocking collectives  163 us (18%)
  matrix products  70.5 us (8%)
  other arithmetic  22.9 us (2%)
  local copies, waits for them, and re-layouts  21.4 us (2%)
  between operations  14.9 us (2%)
    all_gather x1, waiting for transfers between devices, shards(): piece = lax.all_gather(qkv_weight, 'ctx', axis=0, tiled=True)  382 us
    unnamed x1, blocking collectives  163 us
    all_gather x1, waiting for transfers between devices, shards(): key_piece = lax.all_gather(keys, 'ctx', axis=0, tiled=True)  111 us
    all_gather x1, waiting for transfers between devices, shards(): value_piece = lax.all_gather(values, 'ctx', axis=0, tiled=True)  75.6 us
    all_gather x1, waiting for transfers between devices, shards(): gathered = lax.all_gather(normed, 'head', axis=0, tiled=True)  49.5 us
    dot_general x1, matrix products, shards(): jnp.einsum('qhd,khd->hqk', query, key_piece, preferred_element_type=jnp.f...  19 us
  transfers between devices with their start and end apart: 9, of which 6 were waited for; matrix products, arithmetic and copies ran while one was open for 7% of the time, Pallas kernels for 0%

commit v1 on v0

--- a/solution.py
+++ b/solution.py
@@ -79,24 +79,50 @@
     angles = step_index[0].astype(jnp.float32) * freqs
     timing = jnp.concatenate([jnp.cos(angles), jnp.sin(angles)]).astype(jnp.bfloat16)
     mod_share = jnp.dot(timing[None, :], mod_weight, preferred_element_type=jnp.float32)[0]
-    modulation = lax.all_gather(mod_share, ("head", "ctx"), axis=0, tiled=True)
-    scale = modulation[:D]
-    shift = modulation[D:]
-    embedded = jnp.dot(
-        patches,
-        lax.all_gather(patch_weight, ("head", "ctx"), axis=1, tiled=True),
-        preferred_element_type=jnp.float32,
+    modulation = lax.all_gather(
+        lax.all_gather(mod_share, "ctx", axis=0, tiled=True), "head", axis=0, tiled=True
     )
-    inverse = lax.rsqrt(jnp.mean(embedded * embedded, -1, keepdims=True) + 1e-06)
-    normed = (embedded * inverse * (1.0 + scale) + shift).astype(jnp.bfloat16)
-    gathered = lax.all_gather(normed, "head", axis=0, tiled=True)
-    group_rows = gathered.shape[0]
+    n_head = lax.axis_size("head")
+    n_ctx = lax.axis_size("ctx")
+    h_idx = lax.axis_index("head")
+    c_idx = lax.axis_index("ctx")
+    quarter = D // n_head
+    scale = lax.dynamic_slice_in_dim(modulation, h_idx * quarter, quarter)
+    shift = lax.dynamic_slice_in_dim(modulation, D + h_idx * quarter, quarter)
+    weight_quarter = lax.all_gather(patch_weight, "ctx", axis=1, tiled=True)
+    block_patches = lax.all_gather(patches, "head", axis=0, tiled=True)
+    embedded = jnp.dot(block_patches, weight_quarter, preferred_element_type=jnp.float32)
+    squares = lax.all_gather(jnp.sum(embedded * embedded, -1), "head", axis=0, tiled=False)
+    inverse = lax.rsqrt(jnp.sum(squares, 0) / D + 1e-06)[:, None]
+    normed_quarter = (embedded * inverse * (1.0 + scale) + shift).astype(jnp.bfloat16)
+    normed = lax.all_gather(normed_quarter, "head", axis=1, tiled=True)
+    group_rows = normed.shape[0]
     heads_here = qkv_weight.shape[1]
     out_cols = heads_here * 3 * HDIM
-    piece = lax.all_gather(qkv_weight, "ctx", axis=0, tiled=True)
-    qkv = jnp.dot(
-        gathered, piece.reshape(piece.shape[0], out_cols), preferred_element_type=jnp.float32
+    local = qkv_weight.reshape(qkv_weight.shape[0], out_cols)
+    rows = local.shape[0]
+    half_rows = rows // 2
+    core = lax.axis_index("dp") % 2
+    mine = lax.dynamic_slice_in_dim(local, core * half_rows, half_rows, 0)
+    fetched = jnp.stack(
+        [
+            lax.ppermute(mine, "ctx", [(i, (i + s) % n_ctx) for i in range(n_ctx)])
+            for s in range(1, n_ctx)
+        ]
     )
+    n_dp = lax.axis_size("dp")
+    partner = lax.ppermute(fetched, "dp", [(i, i ^ 1) for i in range(n_dp)])
+    weight = jnp.concatenate(
+        [local, fetched.reshape(-1, out_cols), partner.reshape(-1, out_cols)], 0
+    )
+    pieces = [lax.dynamic_slice_in_dim(normed, c_idx * rows, rows, 1)]
+    for side in (core, 1 - core):
+        for s in range(1, n_ctx):
+            block = (c_idx + n_ctx - s) % n_ctx
+            pieces.append(
+                lax.dynamic_slice_in_dim(normed, block * rows + side * half_rows, half_rows, 1)
+            )
+    qkv = jnp.dot(jnp.concatenate(pieces, 1), weight, preferred_element_type=jnp.float32)
     qkv = qkv.astype(jnp.bfloat16).reshape(group_rows, heads_here, 3, HDIM)
     query = qkv[:, :, 0]
     keys = qkv[:, :, 1]

time: 924 us -> 625 us (0.68)
  waiting for transfers between devices: 622 us -> 271 us
  local copies, waits for them, and re-layouts: 21.4 us -> 77 us
  blocking collectives: 163 us -> 133 us
  starting transfers between devices: 8.3 us -> 22.5 us
    all_gather x3 -> x2, waiting for transfers between devices: 431 us -> 70 us  [the longest x1 70 us: shards(): normed = lax.all_gather(normed_quarter, 'head', axis=1, tiled=True)]
    unnamed x1, blocking collectives: 163 us -> 96.2 us
    all_gather x0 -> x3, blocking collectives: none -> 36.9 us  [the longest x1 13.5 us: shards(): block_patches = lax.all_gather(patches, 'head', axis=0, tiled=True)]
    ppermute x0 -> x8, starting transfers between devices: none -> 14.5 us  [the longest x7 14.5 us: shards(): lax.ppermute(mine, 'ctx', [(i, (i + s) % n_ctx) for i in range(n_ctx)])]
    unnamed x24 -> x35, local copies, waits for them, and re-layouts: 8.06 us -> 21.6 us
    dynamic_slice x0 -> x4, local copies, waits for them, and re-layouts: none -> 13.5 us  [the longest x1 8.05 us: shards(): lax.dynamic_slice_in_dim(normed, block * rows + side * half_rows, half_ro...]
  transfers between devices with their start and end apart: 9 -> 16, of which waited for: 6 -> 8; matrix products, arithmetic and copies ran while one was open for 7% -> 20% of each run, Pallas kernels for 0% -> 0%
where the time goes in v1:
time: 625 us; the launch traced here: 616 us
  waiting for transfers between devices  271 us (43%)
  blocking collectives  133 us (21%)
  local copies, waits for them, and re-layouts  77 us (12%)
  matrix products  72 us (12%)
  other arithmetic  25.5 us (4%)
  starting transfers between devices  22.5 us (4%)
  between operations  15.2 us (2%)
    all_gather x1, waiting for transfers between devices, shards(): key_piece = lax.all_gather(keys, 'ctx', axis=0, tiled=True)  110 us
    unnamed x1, blocking collectives  96.2 us
    all_gather x1, waiting for transfers between devices, shards(): value_piece = lax.all_gather(values, 'ctx', axis=0, tiled=True)  75.3 us
    all_gather x1, waiting for transfers between devices, shards(): normed = lax.all_gather(normed_quarter, 'head', axis=1, tiled=True)  70 us
    unnamed x35, local copies, waits for them, and re-layouts  21.6 us
    dot_general x1, matrix products, shards(): jnp.einsum('qhd,khd->hqk', query, key_piece, preferred_element_type=jnp.f...  19.3 us
    dot_general x1, matrix products, shards(): jnp.dot(jnp.concatenate(pieces, 1), weight, preferred_element_type=jnp.fl...  18.2 us
    dot_general x1, matrix products, shards(): jnp.einsum('hqk,khd->hqd', probs.astype(jnp.bfloat16), value_piece, prefe...  17.4 us
  transfers between devices with their start and end apart: 16, of which 8 were waited for; matrix products, arithmetic and copies ran while one was open for 20% of the time, Pallas kernels for 0%

profile of v1, /device:TPU:0, one launch (start us, length us, event | category | flops | bytes accessed | tf_op | source)
XLA Modules:
  0.0 616.0 jit_solution(10998383300142862645)
XLA Ops:
  6.5 3.9 copy.39
  26.6 4.0 collective-permute-start
  35.1 96.2 %all-reduce = f32[2560]{0:T(1024)} all-reduce(f32[2560]{0:T(1024)S(1)} %dynamic-update-slice), channel_id=1, replica_groups=mesh['dp'=4,'head'=4,'ctx'=8] {'ctx'}, use_global_device_ids=true, to_apply=%add | all-reduce | flops 2560 | bytes 20480
  132.0 13.0 %all-gather.4 = f32[4,1,2560]{2,1,0:T(1,128)} all-gather(f32[1,1,2560]{2,1,0:T(1,128)S(1)} %reshape.69), channel_id=1, replica_groups=mesh['dp'=4,'head'=4,'ctx'=8] {'head'}, dimensions={0}, use_global_device_ids=true | all-gather | bytes 51200 | tf_op jit(solution)/shard_map/all_gather | solution.py:82
  155.4 3.6 collective-permute-done.1
  166.0 3.9 collective-permute-done.3
  169.9 4.4 collective-permute-start.8
  184.1 3.4 multiply_convert_fusion
  189.9 3.1 copy.66
  193.0 3.2 reshape.54
  199.7 13.5 %all_gather.27 = bf16[512,768]{1,0:T(8,128)(2,1)S(1)} all-gather(bf16[128,768]{1,0:T(8,128)(2,1)} %reshape.55), channel_id=1, replica_groups=mesh['dp'=4,'head'=4,'ctx'=8] {'head'}, dimensions={0}, use_global_device_ids=true | all-gather | bytes 983040 | tf_op jit(solution)/shard_map/all_gather | solution.py:93
  235.3 4.2 multiply_reduce_fusion.1
  239.5 10.4 %all-gather.3 = f32[4,1,512]{2,1,0:T(1,128)S(1)} all-gather(f32[1,1,512]{2,1,0:T(1,128)S(1)} %bitcast.133), channel_id=2, replica_groups=mesh['dp'=4,'head'=4,'ctx'=8] {'head'}, dimensions={0}, use_global_device_ids=true | all-gather | bytes 10240 | tf_op jit(solution)/shard_map/all_gather | solution.py:95
  249.9 3.2 add_convert_fusion
  253.4 3.2 copy.47
  256.6 70.0 %all-gather.12.cloned.1.call-done = bf16[512,5120]{1,0:T(8,128)(2,1)} async-done(((bf16[512,1280]{1,0:T(8,128)(2,1)}), bf16[512,5120]{1,0:T(8,128)(2,1)}) %all-gather.12.cloned.1.call-update) | async-done | bytes 5242896 | tf_op jit(solution)/shard_map/all_gather | solution.py:98
  327.7 8.1 %constant_dynamic-slice_fusion.1 = (bf16[512,320]{1,0:T(8,128)(2,1)S(1)}, bf16[512,320]{1,0:T(8,128)(2,1)S(1)}, bf16[512,320]{1,0:T(8,128)(2,1)S(1)}, bf16[512,3...) fusion(bf16[512,5120]{1,0:T(8,128)(2,1)} %all-gather.12.cloned., ...), kind=kLoop, calls=%fused_computation.165 | loop fusion | bytes 9175096 | tf_op jit(solution)/shard_map/dynamic_slice | solution.py:123
  335.8 9.1 %concatenate.94 = bf16[512,5120]{1,0:T(8,128)(2,1)} concatenate(bf16[512,640]{1,0:T(8,128)(2,1)S(1)} %constant_dynamic-slice_fusion.15, bf16[512,320]{1,0:T(8,128)(2,1)} %get-tuple-element.18, bf16[512,320]{1,0:T(8,128)(2,1)} %get-tuple-element.17, bf16[512,320]{1,0:T(8,128)(2,1)} %get-tuple-element.16, bf16[512,320]{1,0:T(8,128)(2,1)} %get-tuple-element.15, ...), dimensions={1} | concatenate | bytes 10485760 | tf_op jit(solution)/shard_map/concatenate | solution.py:125
  344.8 18.2 %fusion.13 = bf16[512,1920]{1,0:T(8,128)(2,1)} fusion(bf16[512,5120]{1,0:T(8,128)(2,1)} %concatenate.94, bf16[2240,1920]{1,0:T(8,128)(2,1)} %bitcast.42, bf16[2240,1920]{1,0:T(8,128)(2,1)} %bitcast.41, bf16[640,1920]{1,0:T(8,128)(2,1)} %copy.47), kind=kOutput, calls=%fused_computation.30 | convolution fusion | flops 10126295040 | bytes 26869760 | tf_op jit(solution)/shard_map/dot_general | solution.py:125
  368.3 110.4 %all-gather.14.cloned.1.call-done = bf16[4096,5,1,128]{3,0,1,2:T(8,128)(2,1)} async-done(((bf16[512,5,1,128]{3,0,1,2:T(8,128)(2,1)}), bf16[4096,5,1,128]{3,0,1,2:T(8,128)(2,1)}) %all-gather.14.cloned.1.call-update) | async-done | bytes 5242896 | tf_op jit(solution)/shard_map/all_gather | solution.py:132
  478.7 19.3 %multiply_reduce_fusion = (f32[5,512]{1,0:T(8,128)S(1)}, f32[5,512,4096]{2,1,0:T(8,128)}) fusion(bf16[4096,5,1,128]{3,0,1,2:T(8,128)(2,1)} %all-gather.14.cloned.1.call-done, bf16[512,5,3,128]{0,3,2,1:T(8,128)(2,1)S(1)} %bitcast.127), kind=kOutput, calls=%fused_computation.1 | convolution fusion | flops 2705323520 | bytes 47851520 | tf_op jit(solution)/shard_map/qhd,khd->hqk/dot_general | solution.py:135
  498.0 17.4 %fusion = f32[5,512]{1,0:T(8,128)S(1)} fusion(f32[5,512,4096]{2,1,0:T(8,128)} %get-tuple-element.61, f32[5,512]{1,0:T(8,128)S(1)} %broadcast_maximum_fusion), kind=kLoop, calls=%fused_computation.2 | loop fusion | flops 31454720 | bytes 41963520 | tf_op jit(solution)/shard_map/reduce_sum | solution.py:139
  515.4 75.3 %all-gather.16.cloned.1.call-done = bf16[4096,5,1,128]{0,3,1,2:T(8,128)(2,1)} async-done(((bf16[512,5,1,128]{0,3,1,2:T(8,128)(2,1)}), bf16[4096,5,1,128]{0,3,1,2:T(8,128)(2,1)}) %all-gather.16.cloned.1.call-update) | async-done | bytes 5242896 | tf_op jit(solution)/shard_map/all_gather | solution.py:133
  590.7 17.4 %divide_convert_fusion = bf16[512,5,128]{0,2,1:T(8,128)(2,1)S(1)} fusion(bf16[4096,5,1,128]{0,3,1,2:T(8,128)(2,1)} %all-gather.16.cloned.1.call-done, f32[5,512,4096]{2,1,0:T(8,128)} %get-tuple-element.61, f32[5,512]{1,0:T(8,128)S(1)} %broadcast_maximum_fusion, f32[512,5]{0,1:T(8,128)S(1)} %bitcast.131), kind=kOutput, calls=%fused_computation.90 | convolution fusion | flops 2716467200 | bytes 47861760 | tf_op jit(solution)/shard_map/hqk,khd->hqd/dot_general | solution.py:140
  (105 shorter events, 82.4 us)
Async XLA Ops:
  6.5 189.6 %copy-start = (bf16[768,192]{0,1:T(8,128)(2,1)S(1)}, bf16[768,192]{0,1:T(8,128)(2,1)}, u32[]{:S(2)}) copy-start(bf16[768,192]{0,1:T(8,128)(2,1)} %param.13) | copy-start | bytes 884740
  6.5 228.7 %all-gather.10.cloned.1.call-start = ((), (), s32[]{:S(2)}) async-start(), calls=%async_computation | async-start | bytes 2211840 | tf_op jit(solution)/shard_map/all_gather | solution.py:92
  10.5 12.0 %copy-start.6 = (bf16[2,16,3072]{2,1,0:T(8,128)(2,1)S(1)}, bf16[2,16,3072]{2,1,0:T(8,128)(2,1)}, u32[]{:S(2)}) copy-start(bf16[2,16,3072]{2,1,0:T(8,128)(2,1)} %param.10) | copy-start | bytes 589828
  14.8 198.4 %collective-permute-start.4 = (bf16[320,1920]{1,0:T(8,128)(2,1)}, bf16[320,1920]{1,0:T(8,128)(2,1)}, u32[]{:S(2)}, u32[]{:S(2)}) collective-permute-start(bf16[320,1920]{1,0:T(8,128)(2,1)} %copy.40), channel_id=1, source_target_pairs={{0,1},{1,2},{2,3},{3,4},{4,5},{5,6},{6,7},{7,0},{8,9},{9,10},{10,1... | collective-permute-start | bytes 3686408 | tf_op jit(solution)/shard_map/ppermute | solution.py:109
  16.5 200.7 %collective-permute-start.5 = (bf16[320,1920]{1,0:T(8,128)(2,1)}, bf16[320,1920]{1,0:T(8,128)(2,1)}, u32[]{:S(2)}, u32[]{:S(2)}) collective-permute-start(bf16[320,1920]{1,0:T(8,128)(2,1)} %copy.40), channel_id=1, source_target_pairs={{0,2},{1,3},{2,4},{3,5},{4,6},{5,7},{6,0},{7,1},{8,10},{9,11},{10,... | collective-permute-start | bytes 3686408 | tf_op jit(solution)/shard_map/ppermute | solution.py:109
  18.4 202.2 %collective-permute-start.6 = (bf16[320,1920]{1,0:T(8,128)(2,1)}, bf16[320,1920]{1,0:T(8,128)(2,1)}, u32[]{:S(2)}, u32[]{:S(2)}) collective-permute-start(bf16[320,1920]{1,0:T(8,128)(2,1)} %copy.40), channel_id=1, source_target_pairs={{0,3},{1,4},{2,5},{3,6},{4,7},{5,0},{6,1},{7,2},{8,11},{9,12},{10,... | collective-permute-start | bytes 3686408 | tf_op jit(solution)/shard_map/ppermute | solution.py:109
  21.3 201.7 %collective-permute-start.7 = (bf16[320,1920]{1,0:T(8,128)(2,1)}, bf16[320,1920]{1,0:T(8,128)(2,1)}, u32[]{:S(2)}, u32[]{:S(2)}) collective-permute-start(bf16[320,1920]{1,0:T(8,128)(2,1)} %copy.40), channel_id=1, source_target_pairs={{0,4},{1,5},{2,6},{3,7},{4,0},{5,1},{6,2},{7,3},{8,12},{9,13},{10,... | collective-permute-start | bytes 3686408 | tf_op jit(solution)/shard_map/ppermute | solution.py:109
  22.4 10.0 %copy-start.9 = (u32[128]{0:T(128)S(1)}, u32[128]{0:T(128)}, u32[]{:S(2)}) copy-start(u32[128]{0:T(128)} %constant.137) | copy-start | bytes 1540
  26.6 126.2 %collective-permute-start = (bf16[6,1,32,96]{3,2,1,0:T(8,128)(2,1)}, bf16[6,1,32,96]{3,2,1,0:T(8,128)(2,1)}, u32[]{:S(2)}, u32[]{:S(2)}) collective-permute-start(bf16[6,1,32,96]{3,2,1,0:T(8,128)(2,1)} %get-tuple-element.49), channel_id=1, source_target_pairs={{0,8},{8,16},{16,24},{1,9},{9,17},{17,25},{2,10},{10,18},{18,26},{... | collective-permute-start | bytes 110600 | tf_op jit(solution)/shard_map/ppermute | solution.py:19
  30.6 295.9 %all-gather.12.cloned.1.call-start = ((), (), s32[]{:S(2)}) async-start(), calls=%async_computation.1 | async-start | bytes 6553600 | tf_op jit(solution)/shard_map/all_gather | solution.py:98
  31.6 123.3 %copy-start.2 = (bf16[6,16,32,96]{3,2,1,0:T(8,128)(2,1)S(1)}, bf16[6,16,32,96]{3,2,1,0:T(8,128)(2,1)}, u32[]{:S(2)}) copy-start(bf16[6,16,32,96]{3,2,1,0:T(8,128)(2,1)} %reshape.52) | copy-start | bytes 1769476
  152.8 6.2 %collective-permute-start.1 = (bf16[6,1,32,96]{3,2,1,0:T(8,128)(2,1)}, bf16[6,1,32,96]{3,2,1,0:T(8,128)(2,1)S(1)}, u32[]{:S(2)}, u32[]{:S(2)}) collective-permute-start(bf16[6,1,32,96]{3,2,1,0:T(8,128)(2,1)} %get-tuple-element.48), channel_id=1, source_target_pairs={{8,0},{16,8},{24,16},{9,1},{17,9},{25,17},{10,2},{18,10},{26,18},{... | collective-permute-start | bytes 110600 | tf_op jit(solution)/shard_map/ppermute | solution.py:21
  159.1 3.6 collective-permute-start.2
  162.8 7.2 %collective-permute-start.3 = (bf16[6,18,1,96]{3,2,1,0:T(2,128)(2,1)S(1)}, bf16[6,18,1,96]{3,2,1,0:T(2,128)(2,1)S(1)}, u32[]{:S(2)}, u32[]{:S(2)}) collective-permute-start(bf16[6,18,1,96]{3,2,1,0:T(2,128)(2,1)S(1)} %get-tuple-element.38), channel_id=1, source_target_pairs={{1,0},{2,1},{3,2},{4,3},{5,4},{6,5},{7,6},{9,8},{10,9},{11,10},{12... | collective-permute-start | bytes 62216 | tf_op jit(solution)/shard_map/ppermute | solution.py:21
  166.0 10.5 %copy-start.7 = (bf16[3,3,288,192]{3,2,1,0:T(8,128)(2,1)S(1)}, bf16[3,3,288,192]{3,2,1,0:T(8,128)(2,1)}, u32[]{:S(2)}) copy-start(bf16[3,3,288,192]{3,2,1,0:T(8,128)(2,1)} %param.11) | copy-start | bytes 2985988
  169.9 55.6 %collective-permute-start.8 = (bf16[320,1920]{1,0:T(8,128)(2,1)}, bf16[320,1920]{1,0:T(8,128)(2,1)}, u32[]{:S(2)}, u32[]{:S(2)}) collective-permute-start(bf16[320,1920]{1,0:T(8,128)(2,1)} %copy.40), channel_id=1, source_target_pairs={{0,5},{1,6},{2,7},{3,0},{4,1},{5,2},{6,3},{7,4},{8,13},{9,14},{10,... | collective-permute-start | bytes 3686408 | tf_op jit(solution)/shard_map/ppermute | solution.py:109
  180.0 1.0 copy-start.5
  182.1 1.0 copy-start.3
  213.2 16.9 %collective-permute-start.9 = (bf16[320,1920]{1,0:T(8,128)(2,1)}, bf16[320,1920]{1,0:T(8,128)(2,1)S(1)}, u32[]{:S(2)}, u32[]{:S(2)}) collective-permute-start(bf16[320,1920]{1,0:T(8,128)(2,1)} %copy.40), channel_id=1, source_target_pairs={{0,6},{1,7},{2,0},{3,1},{4,2},{5,3},{6,4},{7,5},{8,14},{9,15},{10,... | collective-permute-start | bytes 3686408 | tf_op jit(solution)/shard_map/ppermute | solution.py:109
  217.2 16.9 %collective-permute-start.10 = (bf16[320,1920]{1,0:T(8,128)(2,1)}, bf16[320,1920]{1,0:T(8,128)(2,1)S(1)}, u32[]{:S(2)}, u32[]{:S(2)}) collective-permute-start(bf16[320,1920]{1,0:T(8,128)(2,1)} %copy.40), channel_id=1, source_target_pairs={{0,7},{1,0},{2,1},{3,2},{4,3},{5,4},{6,5},{7,6},{8,15},{9,8},{10,9... | collective-permute-start | bytes 3686408 | tf_op jit(solution)/shard_map/ppermute | solution.py:109
  235.3 109.6 %collective-permute-start.11 = (bf16[7,320,1920]{2,1,0:T(8,128)(2,1)}, bf16[7,320,1920]{2,1,0:T(8,128)(2,1)}, u32[]{:S(2)}, u32[]{:S(2)}) collective-permute-start(bf16[7,320,1920]{2,1,0:T(8,128)(2,1)} %bitcast_dynamic-update-slice_fusion), channel_id=1, source_target_pairs={{0,32},{32,0},{64,96},{96,64},{1,33},{33,1},{65,97},{97,65},{2,34}... | collective-permute-start | bytes 25804808 | tf_op jit(solution)/shard_map/ppermute | solution.py:114
  253.2 225.5 %all-gather.14.cloned.1.call-start = ((), (), s32[]{:S(2)}) async-start(), calls=%async_computation.2 | async-start | bytes 5898240 | tf_op jit(solution)/shard_map/all_gather | solution.py:132
  367.7 222.9 %all-gather.16.cloned.1.call-start = ((), (), s32[]{:S(2)}) async-start(), calls=%async_computation.3 | async-start | bytes 5898240 | tf_op jit(solution)/shard_map/all_gather | solution.py:133
  590.7 18.5 %copy-start.1 = (bf16[768,192]{0,1:T(8,128)(2,1)S(1)}, bf16[768,192]{0,1:T(8,128)(2,1)}, u32[]{:S(2)}) copy-start(bf16[768,192]{0,1:T(8,128)(2,1)} %param.13) | copy-start | bytes 884740
  (2 other events, 1.9 us)
Sparse Core Ops, SparseCore 0:
  30.8 80.0 all-gather.9
  253.3 73.2 all-gather.11
  367.9 110.7 all-gather.13
  480.2 110.4 all-gather.15

commit v2 on v1

--- a/solution.py
+++ b/solution.py
@@ -23,6 +23,17 @@
             axis=dim,
         )
     return cells
+
+
+def gather_rows(cells, axis):
+    count = lax.axis_size(axis)
+    me = lax.axis_index(axis)
+    parts = [cells] + [
+        lax.ppermute(cells, axis, [(i, (i + s) % count) for i in range(count)])
+        for s in range(1, count)
+    ]
+    stacked = jnp.stack(parts)
+    return jnp.take(stacked, (me - jnp.arange(count)) % count, axis=0)
 
 
 def silu_act(value):
@@ -79,9 +90,7 @@
     angles = step_index[0].astype(jnp.float32) * freqs
     timing = jnp.concatenate([jnp.cos(angles), jnp.sin(angles)]).astype(jnp.bfloat16)
     mod_share = jnp.dot(timing[None, :], mod_weight, preferred_element_type=jnp.float32)[0]
-    modulation = lax.all_gather(
-        lax.all_gather(mod_share, "ctx", axis=0, tiled=True), "head", axis=0, tiled=True
-    )
+    modulation = gather_rows(gather_rows(mod_share, "ctx").reshape(-1), "head").reshape(-1)
     n_head = lax.axis_size("head")
     n_ctx = lax.axis_size("ctx")
     h_idx = lax.axis_index("head")
@@ -90,9 +99,9 @@
     scale = lax.dynamic_slice_in_dim(modulation, h_idx * quarter, quarter)
     shift = lax.dynamic_slice_in_dim(modulation, D + h_idx * quarter, quarter)
     weight_quarter = lax.all_gather(patch_weight, "ctx", axis=1, tiled=True)
-    block_patches = lax.all_gather(patches, "head", axis=0, tiled=True)
+    block_patches = gather_rows(patches, "head").reshape(-1, patches.shape[1])
     embedded = jnp.dot(block_patches, weight_quarter, preferred_element_type=jnp.float32)
-    squares = lax.all_gather(jnp.sum(embedded * embedded, -1), "head", axis=0, tiled=False)
+    squares = gather_rows(jnp.sum(embedded * embedded, -1), "head")
     inverse = lax.rsqrt(jnp.sum(squares, 0) / D + 1e-06)[:, None]
     normed_quarter = (embedded * inverse * (1.0 + scale) + shift).astype(jnp.bfloat16)
     normed = lax.all_gather(normed_quarter, "head", axis=1, tiled=True)

time: 625 us -> 612 us (0.979)
  blocking collectives: 133 us -> 0 us
  waiting for transfers between devices: 271 us -> 336 us
  starting transfers between devices: 22.5 us -> 48.7 us
  local copies, waits for them, and re-layouts: 77 us -> 96.6 us
  other arithmetic: 25.5 us -> 34.4 us
    unnamed x1 -> x0, blocking collectives: 96.2 us -> none
    ppermute x7, waiting for transfers between devices: 5.1 us -> 83.5 us  [shards(): lax.ppermute(mine, 'ctx', [(i, (i + s) % n_ctx) for i in range(n_ctx)])]
    all_gather x3 -> x0, blocking collectives: 36.9 us -> none  [the longest x1 13.5 us: shards(): block_patches = lax.all_gather(patches, 'head', axis=0, tiled=True)]
    ppermute x0 -> x16, starting transfers between devices: none -> 27.7 us  [gather_rows(): lax.ppermute(cells, axis, [(i, (i + s) % count) for i in range(count)])]
    all_gather x1, waiting for transfers between devices: 70 us -> 54.5 us  [shards(): normed = lax.all_gather(normed_quarter, 'head', axis=1, tiled=True)]
    another operation x0 -> x12, local copies, waits for them, and re-layouts: none -> 11.8 us  [gather_rows(): stacked = jnp.stack(parts)]
    ppermute x2, waiting for transfers between devices: 1.77 us -> 11 us  [with_halo(): lax.ppermute(tail, axis, [(i, (i + 1) % count) for i in range(ends)])]
    ppermute x2, waiting for transfers between devices: 7.52 us -> 0.28 us  [with_halo(): lax.ppermute(head, axis, [((i + 1) % count, i) for i in range(ends)])]
  transfers between devices with their start and end apart: 16 -> 32, of which waited for: 8 -> 9; matrix products, arithmetic and copies ran while one was open for 20% -> 27% of each run, Pallas kernels for 0% -> 0%
where the time goes in v2:
time: 612 us; the launch traced here: 602 us
  waiting for transfers between devices  336 us (55%)
  local copies, waits for them, and re-layouts  96.6 us (16%)
  matrix products  71.9 us (12%)
  starting transfers between devices  48.7 us (8%)
  other arithmetic  34.4 us (6%)
  between operations  14.6 us (2%)
    all_gather x1, waiting for transfers between devices, shards(): key_piece = lax.all_gather(keys, 'ctx', axis=0, tiled=True)  110 us
    ppermute x7, waiting for transfers between devices, shards(): lax.ppermute(mine, 'ctx', [(i, (i + s) % n_ctx) for i in range(n_ctx)])  83.5 us
    all_gather x1, waiting for transfers between devices, shards(): value_piece = lax.all_gather(values, 'ctx', axis=0, tiled=True)  75.3 us
    all_gather x1, waiting for transfers between devices, shards(): normed = lax.all_gather(normed_quarter, 'head', axis=1, tiled=True)  54.5 us
    ppermute x16, starting transfers between devices, gather_rows(): lax.ppermute(cells, axis, [(i, (i + s) % count) for i in range(count)])  27.7 us
    unnamed x37, local copies, waits for them, and re-layouts  20.9 us
    dot_general x1, matrix products, shards(): jnp.einsum('qhd,khd->hqk', query, key_piece, preferred_element_type=jnp.f...  19.3 us
    dot_general x1, matrix products, shards(): jnp.dot(jnp.concatenate(pieces, 1), weight, preferred_element_type=jnp.fl...  18.1 us
  transfers between devices with their start and end apart: 32, of which 9 were waited for; matrix products, arithmetic and copies ran while one was open for 27% of the time, Pallas kernels for 0%

profile of v2, /device:TPU:0, one launch (start us, length us, event | category | flops | bytes accessed | tf_op | source)
XLA Modules:
  0.0 601.8 jit_solution(1159484119322378173)
XLA Ops:
  8.4 5.0 collective-permute-start.14
  21.3 3.9 copy.42
  64.0 3.1 collective-permute-start
  80.4 11.0 %collective-permute-done.2 = bf16[6,18,1,96]{3,2,1,0:T(2,128)(2,1)S(1)} collective-permute-done((bf16[6,18,1,96]{3,2,1,0:T(2,128)(2,1)S(1)}, bf16[6,18,1,96]{3,2,1,0:T(2,128)(2,1)S(1)}, u32[]{:S(2)}, u32[]{:S(2)}) %collective-permute-start.2) | collective-permute-done | bytes 20768 | tf_op jit(solution)/shard_map/ppermute | solution.py:19
  103.6 3.5 multiply_convert_fusion
  109.4 3.2 copy.69
  112.6 3.5 reshape.193
  129.2 3.1 collective-permute-start.22
  132.3 3.2 collective-permute-start.23
  149.0 13.2 %collective-permute-done.22 = bf16[320,1920]{1,0:T(8,128)(2,1)} collective-permute-done((bf16[320,1920]{1,0:T(8,128)(2,1)}, bf16[320,1920]{1,0:T(8,128)(2,1)}, u32[]{:S(2)}, u32[]{:S(2)}) %collective-permute-start.22) | collective-permute-done | bytes 1228832 | tf_op jit(solution)/shard_map/ppermute | solution.py:118
  164.7 21.0 %collective-permute-done.23 = bf16[320,1920]{1,0:T(8,128)(2,1)} collective-permute-done((bf16[320,1920]{1,0:T(8,128)(2,1)}, bf16[320,1920]{1,0:T(8,128)(2,1)}, u32[]{:S(2)}, u32[]{:S(2)}) %collective-permute-start.23) | collective-permute-done | bytes 1228832 | tf_op jit(solution)/shard_map/ppermute | solution.py:118
  192.7 47.0 %collective-permute-done.25 = bf16[320,1920]{1,0:T(8,128)(2,1)S(1)} collective-permute-done((bf16[320,1920]{1,0:T(8,128)(2,1)}, bf16[320,1920]{1,0:T(8,128)(2,1)S(1)}, u32[]{:S(2)}, u32[]{:S(2)}) %collective-permute-start.25) | collective-permute-done | bytes 1228832 | tf_op jit(solution)/shard_map/ppermute | solution.py:118
  240.9 4.2 multiply_reduce_fusion.1
  251.5 3.2 add_convert_fusion
  254.9 3.2 copy.50
  258.0 54.5 %all-gather.9.cloned.1.call-done = bf16[512,5120]{1,0:T(8,128)(2,1)} async-done(((bf16[512,1280]{1,0:T(8,128)(2,1)}), bf16[512,5120]{1,0:T(8,128)(2,1)}) %all-gather.9.cloned.1.call-update) | async-done | bytes 5242896 | tf_op jit(solution)/shard_map/all_gather | solution.py:107
  313.7 8.1 %constant_dynamic-slice_fusion.1 = (bf16[512,320]{1,0:T(8,128)(2,1)S(1)}, bf16[512,320]{1,0:T(8,128)(2,1)S(1)}, bf16[512,320]{1,0:T(8,128)(2,1)S(1)}, bf16[512,3...) fusion(bf16[512,5120]{1,0:T(8,128)(2,1)} %all-gather.9.cloned.1, ...), kind=kLoop, calls=%fused_computation.177 | loop fusion | bytes 9175096 | tf_op jit(solution)/shard_map/dynamic_slice | solution.py:132
  321.8 9.1 %concatenate.93 = bf16[512,5120]{1,0:T(8,128)(2,1)} concatenate(bf16[512,640]{1,0:T(8,128)(2,1)S(1)} %constant_dynamic-slice_fusion.15, bf16[512,320]{1,0:T(8,128)(2,1)} %get-tuple-element.18, bf16[512,320]{1,0:T(8,128)(2,1)} %get-tuple-element.17, bf16[512,320]{1,0:T(8,128)(2,1)} %get-tuple-element.16, bf16[512,320]{1,0:T(8,128)(2,1)} %get-tuple-element.15, ...), dimensions={1} | concatenate | bytes 10485760 | tf_op jit(solution)/shard_map/concatenate | solution.py:134
  330.9 18.1 %fusion.13 = bf16[512,1920]{1,0:T(8,128)(2,1)} fusion(bf16[512,5120]{1,0:T(8,128)(2,1)} %concatenate.93, bf16[2240,1920]{1,0:T(8,128)(2,1)} %bitcast.50, bf16[2240,1920]{1,0:T(8,128)(2,1)} %bitcast.49, bf16[640,1920]{1,0:T(8,128)(2,1)} %copy.50), kind=kOutput, calls=%fused_computation.34 | convolution fusion | flops 10126295040 | bytes 26869760 | tf_op jit(solution)/shard_map/dot_general | solution.py:134
  354.3 110.4 %all-gather.11.cloned.1.call-done = bf16[4096,5,1,128]{3,0,1,2:T(8,128)(2,1)} async-done(((bf16[512,5,1,128]{3,0,1,2:T(8,128)(2,1)}), bf16[4096,5,1,128]{3,0,1,2:T(8,128)(2,1)}) %all-gather.11.cloned.1.call-update) | async-done | bytes 5242896 | tf_op jit(solution)/shard_map/all_gather | solution.py:141
  464.7 19.3 %multiply_reduce_fusion = (f32[5,512]{1,0:T(8,128)S(1)}, f32[5,512,4096]{2,1,0:T(8,128)}) fusion(bf16[4096,5,1,128]{3,0,1,2:T(8,128)(2,1)} %all-gather.11.cloned.1.call-done, bf16[512,5,3,128]{0,3,2,1:T(8,128)(2,1)S(1)} %bitcast.139), kind=kOutput, calls=%fused_computation.5 | convolution fusion | flops 2705323520 | bytes 47851520 | tf_op jit(solution)/shard_map/qhd,khd->hqk/dot_general | solution.py:144
  484.0 17.4 %fusion = f32[5,512]{1,0:T(8,128)S(1)} fusion(f32[5,512,4096]{2,1,0:T(8,128)} %get-tuple-element.63, f32[5,512]{1,0:T(8,128)S(1)} %broadcast_maximum_fusion), kind=kLoop, calls=%fused_computation.6 | loop fusion | flops 31454720 | bytes 41963520 | tf_op jit(solution)/shard_map/reduce_sum | solution.py:148
  501.3 75.3 %all-gather.13.cloned.1.call-done = bf16[4096,5,1,128]{0,3,1,2:T(8,128)(2,1)} async-done(((bf16[512,5,1,128]{0,3,1,2:T(8,128)(2,1)}), bf16[4096,5,1,128]{0,3,1,2:T(8,128)(2,1)}) %all-gather.13.cloned.1.call-update) | async-done | bytes 5242896 | tf_op jit(solution)/shard_map/all_gather | solution.py:142
  576.6 17.3 %divide_convert_fusion = bf16[512,5,128]{0,2,1:T(8,128)(2,1)S(1)} fusion(bf16[4096,5,1,128]{0,3,1,2:T(8,128)(2,1)} %all-gather.13.cloned.1.call-done, f32[5,512,4096]{2,1,0:T(8,128)} %get-tuple-element.63, f32[5,512]{1,0:T(8,128)S(1)} %broadcast_maximum_fusion, f32[512,5]{0,1:T(8,128)S(1)} %bitcast.143), kind=kOutput, calls=%fused_computation.94 | convolution fusion | flops 2716467200 | bytes 47861760 | tf_op jit(solution)/shard_map/hqk,khd->hqd/dot_general | solution.py:149
  (167 shorter events, 126.5 us)
Async XLA Ops:
  6.5 234.3 %all-gather.7.cloned.1.call-start = ((), (), s32[]{:S(2)}) async-start(), calls=%async_computation | async-start | bytes 2211840 | tf_op jit(solution)/shard_map/all_gather | solution.py:101
  8.4 21.0 %collective-permute-start.14 = (f32[320]{0:T(512)S(1)}, f32[320]{0:T(512)}, u32[]{:S(2)}, u32[]{:S(2)}) collective-permute-start(f32[320]{0:T(512)S(1)} %get-tuple-element.58), channel_id=1, source_target_pairs={{0,5},{1,6},{2,7},{3,0},{4,1},{5,2},{6,3},{7,4},{8,13},{9,14},{10,... | collective-permute-start | bytes 3848 | tf_op jit(solution)/shard_map/ppermute | solution.py:32
  13.5 16.9 %collective-permute-start.15 = (f32[320]{0:T(512)S(1)}, f32[320]{0:T(512)}, u32[]{:S(2)}, u32[]{:S(2)}) collective-permute-start(f32[320]{0:T(512)S(1)} %get-tuple-element.58), channel_id=1, source_target_pairs={{0,6},{1,7},{2,0},{3,1},{4,2},{5,3},{6,4},{7,5},{8,14},{9,15},{10,... | collective-permute-start | bytes 3848 | tf_op jit(solution)/shard_map/ppermute | solution.py:32
  14.2 24.8 %collective-permute-start.16 = (f32[320]{0:T(512)S(1)}, f32[320]{0:T(512)}, u32[]{:S(2)}, u32[]{:S(2)}) collective-permute-start(f32[320]{0:T(512)S(1)} %get-tuple-element.58), channel_id=1, source_target_pairs={{0,7},{1,0},{2,1},{3,2},{4,3},{5,4},{6,5},{7,6},{8,15},{9,8},{10,9... | collective-permute-start | bytes 3848 | tf_op jit(solution)/shard_map/ppermute | solution.py:32
  14.2 27.0 %collective-permute-start.10 = (f32[320]{0:T(512)S(1)}, f32[320]{0:T(512)}, u32[]{:S(2)}, u32[]{:S(2)}) collective-permute-start(f32[320]{0:T(512)S(1)} %get-tuple-element.58), channel_id=1, source_target_pairs={{0,1},{1,2},{2,3},{3,4},{4,5},{5,6},{6,7},{7,0},{8,9},{9,10},{10,1... | collective-permute-start | bytes 3848 | tf_op jit(solution)/shard_map/ppermute | solution.py:32
  16.2 27.3 %collective-permute-start.11 = (f32[320]{0:T(512)S(1)}, f32[320]{0:T(512)S(1)}, u32[]{:S(2)}, u32[]{:S(2)}) collective-permute-start(f32[320]{0:T(512)S(1)} %get-tuple-element.58), channel_id=1, source_target_pairs={{0,2},{1,3},{2,4},{3,5},{4,6},{5,7},{6,0},{7,1},{8,10},{9,11},{10,... | collective-permute-start | bytes 3848 | tf_op jit(solution)/shard_map/ppermute | solution.py:32
  17.6 295.0 %all-gather.9.cloned.1.call-start = ((), (), s32[]{:S(2)}) async-start(), calls=%async_computation.1 | async-start | bytes 6553600 | tf_op jit(solution)/shard_map/all_gather | solution.py:107
  29.4 14.6 %collective-permute-start.12 = (f32[320]{0:T(512)S(1)}, f32[320]{0:T(512)}, u32[]{:S(2)}, u32[]{:S(2)}) collective-permute-start(f32[320]{0:T(512)S(1)} %get-tuple-element.58), channel_id=1, source_target_pairs={{0,3},{1,4},{2,5},{3,6},{4,7},{5,0},{6,1},{7,2},{8,11},{9,12},{10,... | collective-permute-start | bytes 3848 | tf_op jit(solution)/shard_map/ppermute | solution.py:32
  30.4 14.9 %collective-permute-start.13 = (f32[320]{0:T(512)S(1)}, f32[320]{0:T(512)}, u32[]{:S(2)}, u32[]{:S(2)}) collective-permute-start(f32[320]{0:T(512)S(1)} %get-tuple-element.58), channel_id=1, source_target_pairs={{0,4},{1,5},{2,6},{3,7},{4,0},{5,1},{6,2},{7,3},{8,12},{9,13},{10,... | collective-permute-start | bytes 3848 | tf_op jit(solution)/shard_map/ppermute | solution.py:32
  39.0 103.4 %collective-permute-start.20 = (bf16[320,1920]{1,0:T(8,128)(2,1)}, bf16[320,1920]{1,0:T(8,128)(2,1)}, u32[]{:S(2)}, u32[]{:S(2)}) collective-permute-start(bf16[320,1920]{1,0:T(8,128)(2,1)} %copy.43), channel_id=1, source_target_pairs={{0,1},{1,2},{2,3},{3,4},{4,5},{5,6},{6,7},{7,0},{8,9},{9,10},{10,1... | collective-permute-start | bytes 3686408 | tf_op jit(solution)/shard_map/ppermute | solution.py:118
  41.2 104.7 %collective-permute-start.21 = (bf16[320,1920]{1,0:T(8,128)(2,1)}, bf16[320,1920]{1,0:T(8,128)(2,1)}, u32[]{:S(2)}, u32[]{:S(2)}) collective-permute-start(bf16[320,1920]{1,0:T(8,128)(2,1)} %copy.43), channel_id=1, source_target_pairs={{0,2},{1,3},{2,4},{3,5},{4,6},{5,7},{6,0},{7,1},{8,10},{9,11},{10,... | collective-permute-start | bytes 3686408 | tf_op jit(solution)/shard_map/ppermute | solution.py:118
  50.0 14.0 %collective-permute-start.17 = (f32[2560]{0:T(1024)}, f32[2560]{0:T(1024)}, u32[]{:S(2)}, u32[]{:S(2)}) collective-permute-start(f32[2560]{0:T(1024)} %select_n.224), channel_id=1, source_target_pairs={{0,8},{8,16},{16,24},{24,0},{1,9},{9,17},{17,25},{25,1},{2,10},{10... | collective-permute-start | bytes 30728 | tf_op jit(solution)/shard_map/ppermute | solution.py:32
  51.5 16.3 %collective-permute-start.18 = (f32[2560]{0:T(1024)}, f32[2560]{0:T(1024)}, u32[]{:S(2)}, u32[]{:S(2)}) collective-permute-start(f32[2560]{0:T(1024)} %select_n.224), channel_id=1, source_target_pairs={{0,16},{8,24},{16,0},{24,8},{1,17},{9,25},{17,1},{25,9},{2,18},{10... | collective-permute-start | bytes 30728 | tf_op jit(solution)/shard_map/ppermute | solution.py:32
  54.2 15.6 %collective-permute-start.19 = (f32[2560]{0:T(1024)}, f32[2560]{0:T(1024)}, u32[]{:S(2)}, u32[]{:S(2)}) collective-permute-start(f32[2560]{0:T(1024)} %select_n.224), channel_id=1, source_target_pairs={{0,24},{8,0},{16,8},{24,16},{1,25},{9,1},{17,9},{25,17},{2,26},{10... | collective-permute-start | bytes 30728 | tf_op jit(solution)/shard_map/ppermute | solution.py:32
  76.1 15.2 %collective-permute-start.2 = (bf16[6,18,1,96]{3,2,1,0:T(2,128)(2,1)S(1)}, bf16[6,18,1,96]{3,2,1,0:T(2,128)(2,1)S(1)}, u32[]{:S(2)}, u32[]{:S(2)}) collective-permute-start(bf16[6,18,1,96]{3,2,1,0:T(2,128)(2,1)S(1)} %get-tuple-element.37), channel_id=1, source_target_pairs={{0,1},{1,2},{2,3},{3,4},{4,5},{5,6},{6,7},{8,9},{9,10},{10,11},{11... | collective-permute-start | bytes 62216 | tf_op jit(solution)/shard_map/ppermute | solution.py:19
  78.5 15.3 %collective-permute-start.3 = (bf16[6,18,1,96]{3,2,1,0:T(2,128)(2,1)S(1)}, bf16[6,18,1,96]{3,2,1,0:T(2,128)(2,1)S(1)}, u32[]{:S(2)}, u32[]{:S(2)}) collective-permute-start(bf16[6,18,1,96]{3,2,1,0:T(2,128)(2,1)S(1)} %get-tuple-element.38), channel_id=1, source_target_pairs={{1,0},{2,1},{3,2},{4,3},{5,4},{6,5},{7,6},{9,8},{10,9},{11,10},{12... | collective-permute-start | bytes 62216 | tf_op jit(solution)/shard_map/ppermute | solution.py:21
  129.2 33.0 %collective-permute-start.22 = (bf16[320,1920]{1,0:T(8,128)(2,1)}, bf16[320,1920]{1,0:T(8,128)(2,1)}, u32[]{:S(2)}, u32[]{:S(2)}) collective-permute-start(bf16[320,1920]{1,0:T(8,128)(2,1)} %copy.43), channel_id=1, source_target_pairs={{0,3},{1,4},{2,5},{3,6},{4,7},{5,0},{6,1},{7,2},{8,11},{9,12},{10,... | collective-permute-start | bytes 3686408 | tf_op jit(solution)/shard_map/ppermute | solution.py:118
  132.3 53.4 %collective-permute-start.23 = (bf16[320,1920]{1,0:T(8,128)(2,1)}, bf16[320,1920]{1,0:T(8,128)(2,1)}, u32[]{:S(2)}, u32[]{:S(2)}) collective-permute-start(bf16[320,1920]{1,0:T(8,128)(2,1)} %copy.43), channel_id=1, source_target_pairs={{0,4},{1,5},{2,6},{3,7},{4,0},{5,1},{6,2},{7,3},{8,12},{9,13},{10,... | collective-permute-start | bytes 3686408 | tf_op jit(solution)/shard_map/ppermute | solution.py:118
  135.5 54.9 %collective-permute-start.24 = (bf16[320,1920]{1,0:T(8,128)(2,1)}, bf16[320,1920]{1,0:T(8,128)(2,1)}, u32[]{:S(2)}, u32[]{:S(2)}) collective-permute-start(bf16[320,1920]{1,0:T(8,128)(2,1)} %copy.43), channel_id=1, source_target_pairs={{0,5},{1,6},{2,7},{3,0},{4,1},{5,2},{6,3},{7,4},{8,13},{9,14},{10,... | collective-permute-start | bytes 3686408 | tf_op jit(solution)/shard_map/ppermute | solution.py:118
  142.4 97.3 %collective-permute-start.25 = (bf16[320,1920]{1,0:T(8,128)(2,1)}, bf16[320,1920]{1,0:T(8,128)(2,1)S(1)}, u32[]{:S(2)}, u32[]{:S(2)}) collective-permute-start(bf16[320,1920]{1,0:T(8,128)(2,1)} %copy.43), channel_id=1, source_target_pairs={{0,6},{1,7},{2,0},{3,1},{4,2},{5,3},{6,4},{7,5},{8,14},{9,15},{10,... | collective-permute-start | bytes 3686408 | tf_op jit(solution)/shard_map/ppermute | solution.py:118
  146.0 102.4 %collective-permute-start.26 = (bf16[320,1920]{1,0:T(8,128)(2,1)}, bf16[320,1920]{1,0:T(8,128)(2,1)}, u32[]{:S(2)}, u32[]{:S(2)}) collective-permute-start(bf16[320,1920]{1,0:T(8,128)(2,1)} %copy.43), channel_id=1, source_target_pairs={{0,7},{1,0},{2,1},{3,2},{4,3},{5,4},{6,5},{7,6},{8,15},{9,8},{10,9... | collective-permute-start | bytes 3686408 | tf_op jit(solution)/shard_map/ppermute | solution.py:118
  250.8 80.1 %collective-permute-start.27 = (bf16[7,320,1920]{2,1,0:T(8,128)(2,1)}, bf16[7,320,1920]{2,1,0:T(8,128)(2,1)}, u32[]{:S(2)}, u32[]{:S(2)}) collective-permute-start(bf16[7,320,1920]{2,1,0:T(8,128)(2,1)} %bitcast_dynamic-update-slice_fusion), channel_id=1, source_target_pairs={{0,32},{32,0},{64,96},{96,64},{1,33},{33,1},{65,97},{97,65},{2,34}... | collective-permute-start | bytes 25804808 | tf_op jit(solution)/shard_map/ppermute | solution.py:123
  254.7 210.0 %all-gather.11.cloned.1.call-start = ((), (), s32[]{:S(2)}) async-start(), calls=%async_computation.2 | async-start | bytes 5898240 | tf_op jit(solution)/shard_map/all_gather | solution.py:141
  353.7 222.9 %all-gather.13.cloned.1.call-start = ((), (), s32[]{:S(2)}) async-start(), calls=%async_computation.3 | async-start | bytes 5898240 | tf_op jit(solution)/shard_map/all_gather | solution.py:142
  (21 other events, 261.5 us)
Sparse Core Ops, SparseCore 0:
  17.7 74.1 all-gather.6
  254.8 57.7 all-gather.8
  353.9 110.7 all-gather.10
  466.2 110.4 all-gather.12
